TPU v7x, 32 devices: a whole 2x2x4 slice. The times are simulated.
32 devices in a mesh: dp: 8 (over z, y), mp: 4 (over x, core).
Axes of the slice: x: 2, y: 2, z: 4, core: 2. Of those that a mesh axis runs over, the one named last changes fastest.
Arguments:
- gradients: bfloat16 [8, 4, 192, 16384], P('dp', 'mp'), may hold values from -3000 to 3000
- owner_list: int32 [192], replicated, may hold values from 0 to 7, as said below
- master_weights: float32 [4, 288, 16384], P('mp', 'dp'), may hold values from -6 to 6
- first_moment: float32 [4, 288, 16384], P('mp', 'dp'), may hold values from -6 to 6
- second_moment: float32 [4, 288, 16384], P('mp', 'dp'), may hold values from 0.05 to 2
- average_weights: float32 [4, 288, 16384], P('mp', 'dp'), may hold values from -6 to 6
Outputs:
- new_params: bfloat16 [4, 192, 16384], P('mp')
- new_master: float32 [4, 288, 16384], P('mp', 'dp')
- new_first: float32 [4, 288, 16384], P('mp', 'dp')
- new_second: float32 [4, 288, 16384], P('mp', 'dp')
- average_rows: float32 [4, 192, 16384], P('mp', 'dp')
Inputs may be any that keep to these rules, and one draw needn't show every extreme that they name: `owner_list`: each data rank owns at most 36 segments, and some rank owns exactly 36.
All inputs are finite; a program needn't handle non-finite values.
Results may differ from a plain program's by a relative error of at most 0.015.
Values may be sent and summed in bfloat16 or wider, within the bound.
No kernel may reach another device: no remote copies, remote signals or barrier semaphores. Data moves between devices by JAX's collectives and lax.ppermute only.
A program may use at most 128 MiB of HBM per device.

v0:
```python
import math
import jax
import jax.numpy as jnp
from jax import lax
from jax.sharding import PartitionSpec as P


def slot_matrix(owner_list, ranks, cap):
    count = owner_list.shape[0]
    position = jnp.arange(count, dtype=jnp.int32)
    same_owner = (owner_list[:, None] == owner_list[None, :]) & (
        position[None, :] < position[:, None]
    )
    slot_index = owner_list * cap + jnp.sum(same_owner.astype(jnp.int32), axis=1)
    rows = jnp.arange(ranks * cap, dtype=jnp.int32)
    return (rows[:, None] == slot_index[None, :]).astype(jnp.float32)


def on_device(gradients, owner_list, master_weights, first_moment, second_moment, average_weights):
    highest = lax.Precision.HIGHEST
    local_grad = gradients[0, 0]
    nseg, seg = local_grad.shape
    cap = master_weights.shape[1]
    ranks = lax.axis_size("dp")
    blocks = lax.axis_size("mp")
    per_rank = nseg // ranks
    my_rank = lax.axis_index("dp")
    placing = slot_matrix(owner_list, ranks, cap)
    my_slots = lax.dynamic_slice_in_dim(placing, my_rank * cap, cap, 0)
    in_use = jnp.sum(my_slots, axis=1)[:, None]
    summed = lax.psum(local_grad.astype(jnp.float32).astype(jnp.bfloat16), "dp").astype(jnp.float32)
    total_sq = lax.psum(jnp.sum(summed * summed), "mp")
    owned_grad = jnp.dot(my_slots, summed, precision=highest)
    clip_factor = jnp.minimum(1.0, math.sqrt(blocks * nseg * seg) / (jnp.sqrt(total_sq) + 1e-06))
    owned_grad = clip_factor * owned_grad
    new_first = in_use * (0.9 * first_moment[0] + 0.1 * owned_grad)
    new_second = in_use * (0.95 * second_moment[0] + 0.05 * owned_grad * owned_grad)
    first_hat = new_first / (1.0 - 0.9**20)
    second_hat = new_second / (1.0 - 0.95**20)
    old_master = master_weights[0]
    new_master = in_use * (
        old_master - 0.02 * (first_hat / (jnp.sqrt(second_hat) + 1e-08) + 0.1 * old_master)
    )
    averaged = 0.9 * average_weights[0] + 0.1 * new_master
    placing_rows = placing.T
    placing_half = placing_rows.astype(jnp.bfloat16)
    gathered = jnp.dot(
        placing_half,
        lax.all_gather(new_master.astype(jnp.bfloat16), "dp", axis=0, tiled=True),
        preferred_element_type=jnp.float32,
    )
    new_params = gathered.astype(jnp.bfloat16)
    spread_out = jnp.dot(my_slots.T, averaged, precision=highest).reshape(ranks, per_rank, seg)
    arrived = lax.all_to_all(spread_out, "dp", split_axis=0, concat_axis=0, tiled=True)
    average_rows = jnp.sum(arrived, axis=0)
    return (
        new_params[None],
        new_master[None],
        new_first[None],
        new_second[None],
        average_rows[None],
    )


def solution(mesh):
    return jax.shard_map(
        on_device,
        mesh=mesh,
        in_specs=(
            P("dp", "mp", None, None),
            P(),
            P("mp", "dp", None),
            P("mp", "dp", None),
            P("mp", "dp", None),
            P("mp", "dp", None),
        ),
        out_specs=(
            P("mp", None, None),
            P("mp", "dp", None),
            P("mp", "dp", None),
            P("mp", "dp", None),
            P("mp", "dp", None),
        ),
        check_vma=False,
    )
```

profile of v0, /device:TPU:0, one launch (start us, length us, event | category | flops | bytes accessed | tf_op | source)
XLA Modules:
  0.0 680.6 jit_solution(15627968808862761865)
XLA Ops:
  7.2 0.0 all-reduce.2.cloned.1.call-start
  7.2 0.0 copy-start.3
  7.2 0.7 all-reduce.2.cloned.1.call-update
  7.9 0.0 copy-done.3
  7.9 0.2 convert_reduce_fusion
  8.2 217.6 %all-reduce.2.cloned.1.call-done = bf16[192,16384]{1,0:T(8,128)(2,1)} async-done(((bf16[192,16384]{1,0:T(8,128)(2,1)}), bf16[192,16384]{1,0:T(8,128)(2,1)}) %all-reduce.2.cloned.1.call-update) | async-done | bytes 6291472 | tf_op jit(solution)/shard_map/psum | solution.py:31
  225.8 6.6 multiply_reduce_fusion
  232.4 0.1 convert_reduce_fusion.1
  232.5 7.7 %psum.15 = f32[]{:T(128)} all-reduce(f32[]{:T(128)} %multiply_reduce_fusion), channel_id=1, replica_groups=mesh['dp'=8,'mp'=4] {'mp'}, use_global_device_ids=true, to_apply=%region_4.0 | all-reduce | flops 1 | bytes 8 | tf_op jit(solution)/shard_map/psum | solution.py:32
  240.9 0.0 copy-start
  240.9 14.0 %convert_bitcast_fusion = (bf16[1,36,16384]{2,1,0:T(8,128)(2,1)}, f32[36,16384]{1,0:T(8,128)S(1)}, f32[1,36,16384]{2,1,0:T(8,128)}, f32[1,36,16384]{2,1,0:T(8,128)}) fusion(f32[1,36,16384]{2,0,1:T(1,128)} %param.10, f32[1,36,16384]{2,0,1:T(1,128)} %param.9, f32[1,36,16384]{2,0,1:T(1,128)} %param.8, f32[36]{0:T(128)S(1)} %convert_reduce_fusion.1, ...), kind=kOutput, calls=%fused_computation.20 | convolution fusion | flops 238288896 | bytes 21637640 | tf_op jit(solution)/shard_map/dot_general | solution.py:33
  254.9 0.0 copy-done
  254.9 8.4 %fusion.6 = f32[192,16384]{1,0:T(8,128)} fusion(f32[1,36,16384]{2,0,1:T(1,128)S(1)} %copy-done, f32[36,16384]{1,0:T(8,128)S(1)} %get-tuple-element.26, pred[288,192]{1,0:T(8,128)(4,1)S(1)} %iota_compare_fusion, s32[]{:T(128)S(6)} %select_n.3), kind=kOutput, calls=%fused_computation.13 | convolution fusion | flops 1360723968 | bytes 17573892 | tf_op jit(solution)/shard_map/dot_general | solution.py:53
  263.4 5.3 all-to-all-start
  268.7 0.3 all-gather.3.cloned.1.call-start
  269.0 0.5 all-gather.3.cloned.1.call-update
  269.5 3.8 copy.32
  273.3 3.8 copy.33
  277.2 3.8 copy.34
  281.0 362.5 %all-gather.3.cloned.1.call-done = bf16[8,36,16384]{2,1,0:T(8,128)(2,1)} async-done(((bf16[1,36,16384]{2,1,0:T(8,128)(2,1)}), bf16[8,36,16384]{2,1,0:T(8,128)(2,1)}) %all-gather.3.cloned.1.call-update) | async-done | bytes 9437200 | tf_op jit(solution)/shard_map/all_gather | solution.py:49
  643.5 8.5 %reshape.25 = bf16[288,16384]{1,0:T(8,128)(2,1)} reshape(bf16[8,36,16384]{2,1,0:T(8,128)(2,1)} %all-gather.3.cloned.1.call-done) | data formatting | bytes 18874368
  652.0 9.9 %fusion = bf16[1,192,16384]{2,1,0:T(8,128)(2,1)} fusion(bf16[288,16384]{1,0:T(8,128)(2,1)} %reshape.25, s32[192]{0:T(256)S(1)} %multiply_add_fusion), kind=kOutput, calls=%fused_computation.1 | convolution fusion | flops 1815250944 | bytes 15729408 | tf_op jit(solution)/shard_map/dot_general | solution.py:47
  661.8 5.4 all-to-all-done
  667.2 6.5 reduce_sum.39
  (6 shorter events, 0.1 us)
Async XLA Ops:
  7.2 218.6 %all-reduce.2.cloned.1.call-start = ((), (), s32[]{:S(2)}) async-start(), calls=%async_computation.1 | async-start | bytes 12582912 | tf_op jit(solution)/shard_map/psum | solution.py:31
  7.2 0.7 copy-start.3
  240.9 14.0 %copy-start = (f32[1,36,16384]{2,0,1:T(1,128)S(1)}, f32[1,36,16384]{2,0,1:T(1,128)}, u32[]{:S(2)}) copy-start(f32[1,36,16384]{2,0,1:T(1,128)} %param.11) | copy-start | bytes 7077892
  263.4 403.8 %all-to-all-start = ((f32[8,24,16384]{2,1,0:T(8,128)}), f32[8,24,16384]{2,1,0:T(8,128)}, u32[]{:S(2)}, u32[]{:S(2)}) async-start(f32[8,24,16384]{2,1,0:T(8,128)} %bitcast.45), calls=%async_computation | async-start | bytes 25165824 | tf_op jit(solution)/shard_map/all_to_all | solution.py:54
  268.7 374.8 %all-gather.3.cloned.1.call-start = ((), (), s32[]{:S(2)}) async-start(), calls=%async_computation.2 | async-start | bytes 11796480 | tf_op jit(solution)/shard_map/all_gather | solution.py:49
  269.5 3.8 copy-start.2
  273.3 3.8 copy-start.1
Sparse Core Ops, SparseCore 0:
  11.8 213.9 all-reduce.1
  272.6 370.8 all-gather.2
where the time goes:
time: 681 us
  waiting for transfers between devices  587 us (86%)
  matrix products  32.3 us (5%)
  local copies, waits for them, and re-layouts  20 us (3%)
  between operations  14.8 us (2%)
  other arithmetic  13.5 us (2%)
  blocking collectives  7.68 us (1%)
    all_gather x1, waiting for transfers between devices, on_device(): lax.all_gather(new_master.astype(jnp.bfloat16), 'dp', axis=0, tiled=True)  362 us
    psum x1, waiting for transfers between devices, on_device(): lax.psum(local_grad.astype(jnp.float32).astype(jnp.bfloat16), 'dp')  218 us
    unnamed x12, local copies, waits for them, and re-layouts  20 us
    dot_general x1, matrix products, on_device(): owned_grad = jnp.dot(my_slots, summed, precision=highest)  14 us
  transfers between devices with their start and end apart: 3, of which 3 were waited for; matrix products, arithmetic and copies ran while one was open for 4% of the time, Pallas kernels for 0%

commit v1 on v0

--- a/solution.py
+++ b/solution.py
@@ -3,6 +3,22 @@
 import jax.numpy as jnp
 from jax import lax
 from jax.sharding import PartitionSpec as P
+
+
+def gather_around(x, axis, dim):
+    ways, here, lap = (lax.axis_size(axis), lax.axis_index(axis), x.shape[dim])
+    dims = [n * ways if d == dim else n for d, n in enumerate(x.shape)]
+    full = lax.dynamic_update_slice_in_dim(jnp.zeros(dims, x.dtype), x, here * lap, axis=dim)
+    going_up = going_down = x
+    for far in range(1, ways // 2 + 1):
+        going_up = lax.ppermute(going_up, axis, [(d, (d + 1) % ways) for d in range(ways)])
+        full = lax.dynamic_update_slice_in_dim(full, going_up, (here - far) % ways * lap, axis=dim)
+        if 2 * far < ways:
+            going_down = lax.ppermute(going_down, axis, [(d, (d - 1) % ways) for d in range(ways)])
+            full = lax.dynamic_update_slice_in_dim(
+                full, going_down, (here + far) % ways * lap, axis=dim
+            )
+    return full
 
 
 def slot_matrix(owner_list, ranks, cap):
@@ -46,7 +62,7 @@
     placing_half = placing_rows.astype(jnp.bfloat16)
     gathered = jnp.dot(
         placing_half,
-        lax.all_gather(new_master.astype(jnp.bfloat16), "dp", axis=0, tiled=True),
+        gather_around(new_master.astype(jnp.bfloat16), "dp", 0),
         preferred_element_type=jnp.float32,
     )
     new_params = gathered.astype(jnp.bfloat16)

time: 681 us -> 792 us (1.16)
  the two profiles are of different devices: /device:TPU:0 before, /device:TPU:10 now
where the time goes in v1:
time: 792 us; the launch traced here: 790 us
  waiting for transfers between devices  556 us (70%)
  local copies, waits for them, and re-layouts  84.1 us (11%)
  starting transfers between devices  82.3 us (10%)
  matrix products  32.4 us (4%)
  between operations  14.9 us (2%)
  other arithmetic  13.5 us (2%)
    ppermute x4, waiting for transfers between devices, gather_around(): lax.ppermute(going_up, axis, [(d, (d + 1) % ways) for d in range(ways)])  341 us
    psum x1, waiting for transfers between devices, on_device(): lax.psum(local_grad.astype(jnp.float32).astype(jnp.bfloat16), 'dp')  214 us
    ppermute x4, starting transfers between devices, gather_around(): lax.ppermute(going_up, axis, [(d, (d + 1) % ways) for d in range(ways)])  73 us
    dynamic_update_slice x4, local copies, waits for them, and re-layouts, gather_around(): lax.dynamic_update_slice_in_dim(full, going_up, (here - far) % ways * lap...  33.1 us
    dynamic_update_slice x3, local copies, waits for them, and re-layouts, gather_around(): lax.dynamic_update_slice_in_dim(full, going_down, (here + far) % ways * l...  25.1 us
  transfers between devices with their start and end apart: 9, of which 4 were waited for; matrix products, arithmetic and copies ran while one was open for 12% of the time, Pallas kernels for 0%

profile of v1, /device:TPU:10, one launch (start us, length us, event | category | flops | bytes accessed | tf_op | source)
XLA Modules:
  0.0 790.2 jit_solution(17023939494790311582)
XLA Ops:
  8.2 214.5 %all-reduce.2.cloned.1.call-done = bf16[192,16384]{1,0:T(8,128)(2,1)} async-done(((bf16[192,16384]{1,0:T(8,128)(2,1)}), bf16[192,16384]{1,0:T(8,128)(2,1)}) %all-reduce.2.cloned.1.call-update) | async-done | bytes 6291472 | tf_op jit(solution)/shard_map/psum | solution.py:47
  222.6 6.6 multiply_reduce_fusion
  229.4 6.7 psum.15
  236.9 14.0 %fusion.21 = (bf16[36,16384]{1,0:T(8,128)(2,1)}, f32[36,16384]{1,0:T(8,128)S(1)}, f32[1,36,16384]{2,1,0:T(8,128)}, f32[1,36,16384]{2,1,0:T(8,128)}) fusion(f32[1,36,16384]{2,0,1:T(1,128)} %param.10, f32[1,36,16384]{2,0,1:T(1,128)} %param.9, f32[1,36,16384]{2,0,1:T(1,128)} %param.8, f32[36]{0:T(128)S(1)} %convert_reduce_fusion.1, ...), kind=kOutput, calls=%fused_computation.39 | convolution fusion | flops 238288896 | bytes 21637640 | tf_op jit(solution)/shard_map/dot_general | solution.py:49
  250.9 8.5 %fusion.6 = f32[192,16384]{1,0:T(8,128)} fusion(f32[1,36,16384]{2,0,1:T(1,128)S(1)} %copy-done, f32[36,16384]{1,0:T(8,128)S(1)} %get-tuple-element.16, pred[288,192]{1,0:T(8,128)(4,1)S(1)} %iota_compare_fusion, s32[]{:T(128)S(6)} %select_n.56), kind=kOutput, calls=%fused_computation.13 | convolution fusion | flops 1360723968 | bytes 17573892 | tf_op jit(solution)/shard_map/dot_general | solution.py:69
  259.4 7.4 all-to-all-start
  269.7 229.9 %collective-permute-done = bf16[36,16384]{1,0:T(8,128)(2,1)S(1)} collective-permute-done((bf16[36,16384]{1,0:T(8,128)(2,1)}, bf16[36,16384]{1,0:T(8,128)(2,1)S(1)}, u32[]{:S(2)}, u32[]{:S(2)}) %collective-permute-start) | collective-permute-done | bytes 1179680 | tf_op jit(solution)/shard_map/ppermute | solution.py:14
  500.6 66.5 %collective-permute-start.2 = (bf16[36,16384]{1,0:T(8,128)(2,1)S(1)}, bf16[36,16384]{1,0:T(8,128)(2,1)S(1)}, u32[]{:S(2)}, u32[]{:S(2)}) collective-permute-start(bf16[36,16384]{1,0:T(8,128)(2,1)S(1)} %collective-permute-done), channel_id=1, source_target_pairs={{0,4},{4,8},{8,12},{12,16},{16,20},{20,24},{24,28},{28,0},{1,5},{5... | collective-permute-start | bytes 3538952 | tf_op jit(solution)/shard_map/ppermute | solution.py:14
  567.1 56.3 %collective-permute-done.2 = bf16[36,16384]{1,0:T(8,128)(2,1)S(1)} collective-permute-done((bf16[36,16384]{1,0:T(8,128)(2,1)S(1)}, bf16[36,16384]{1,0:T(8,128)(2,1)S(1)}, u32[]{:S(2)}, u32[]{:S(2)}) %collective-permute-start.2) | collective-permute-done | bytes 1179680 | tf_op jit(solution)/shard_map/ppermute | solution.py:14
  626.3 55.0 %collective-permute-done.4 = bf16[36,16384]{1,0:T(8,128)(2,1)} collective-permute-done((bf16[36,16384]{1,0:T(8,128)(2,1)S(1)}, bf16[36,16384]{1,0:T(8,128)(2,1)}, u32[]{:S(2)}, u32[]{:S(2)}) %collective-permute-start.4) | collective-permute-done | bytes 1179680 | tf_op jit(solution)/shard_map/ppermute | solution.py:14
  683.9 4.7 broadcast_in_dim.12
  688.6 8.6 %dynamic_update_slice.24 = bf16[288,16384]{1,0:T(8,128)(2,1)} dynamic-update-slice(bf16[288,16384]{1,0:T(8,128)(2,1)} %broadcast_in_dim.12, bf16[36,16384]{1,0:T(8,128)(2,1)} %get-tuple-element.15, s32[]{:T(128)S(6)} %select_n.56, s32[]{:T(128)} %constant.66.clone.1) | dynamic-update-slice | bytes 2359300 | tf_op jit(solution)/shard_map/dynamic_update_slice | solution.py:11
  697.2 3.8 copy.20
  701.0 3.8 copy.21
  704.8 3.8 copy.22
  708.7 8.7 %dynamic_update_slice.25 = bf16[288,16384]{1,0:T(8,128)(2,1)} dynamic-update-slice(bf16[288,16384]{1,0:T(8,128)(2,1)} %dynamic_update_slice.24, bf16[36,16384]{1,0:T(8,128)(2,1)} %copy-done.3, s32[]{:T(128)S(6)} %select_n.58, s32[]{:T(128)} %constant.66.clone.1) | dynamic-update-slice | bytes 2359300 | tf_op jit(solution)/shard_map/dynamic_update_slice | solution.py:15
  717.4 8.0 %dynamic_update_slice.26 = bf16[288,16384]{1,0:T(8,128)(2,1)} dynamic-update-slice(bf16[288,16384]{1,0:T(8,128)(2,1)} %dynamic_update_slice.25, bf16[36,16384]{1,0:T(8,128)(2,1)S(1)} %copy-done.5, s32[]{:T(128)S(6)} %select_n.60, s32[]{:T(128)} %constant.66.clone.1) | dynamic-update-slice | bytes 2359300 | tf_op jit(solution)/shard_map/dynamic_update_slice | solution.py:18
  725.4 8.0 %dynamic_update_slice.27 = bf16[288,16384]{1,0:T(8,128)(2,1)} dynamic-update-slice(bf16[288,16384]{1,0:T(8,128)(2,1)} %dynamic_update_slice.26, bf16[36,16384]{1,0:T(8,128)(2,1)S(1)} %copy-done.7, s32[]{:T(128)S(6)} %select_n.62, s32[]{:T(128)} %constant.66.clone.1) | dynamic-update-slice | bytes 2359300 | tf_op jit(solution)/shard_map/dynamic_update_slice | solution.py:15
  733.3 8.6 %dynamic_update_slice.28 = bf16[288,16384]{1,0:T(8,128)(2,1)} dynamic-update-slice(bf16[288,16384]{1,0:T(8,128)(2,1)} %dynamic_update_slice.27, bf16[36,16384]{1,0:T(8,128)(2,1)} %collective-permute-done.3, s32[]{:T(128)S(6)} %select_n.64, s32[]{:T(128)} %constant.66.clone.1) | dynamic-update-slice | bytes 2359300 | tf_op jit(solution)/shard_map/dynamic_update_slice | solution.py:18
  741.9 7.9 dynamic_update_slice.29
  749.8 8.6 %dynamic_update_slice.30 = bf16[288,16384]{1,0:T(8,128)(2,1)} dynamic-update-slice(bf16[288,16384]{1,0:T(8,128)(2,1)} %dynamic_update_slice.29, bf16[36,16384]{1,0:T(8,128)(2,1)} %collective-permute-done.5, s32[]{:T(128)S(6)} %select_n.68, s32[]{:T(128)} %constant.66.clone.1) | dynamic-update-slice | bytes 2359300 | tf_op jit(solution)/shard_map/dynamic_update_slice | solution.py:18
  758.4 8.6 %dynamic_update_slice.31 = bf16[288,16384]{1,0:T(8,128)(2,1)} dynamic-update-slice(bf16[288,16384]{1,0:T(8,128)(2,1)} %dynamic_update_slice.30, bf16[36,16384]{1,0:T(8,128)(2,1)} %collective-permute-done.6, s32[]{:T(128)S(6)} %select_n.70, s32[]{:T(128)} %constant.66.clone.1) | dynamic-update-slice | bytes 2359300 | tf_op jit(solution)/shard_map/dynamic_update_slice | solution.py:15
  767.0 9.9 %fusion = bf16[1,192,16384]{2,1,0:T(8,128)(2,1)} fusion(bf16[288,16384]{1,0:T(8,128)(2,1)} %dynamic_update_slice.31, s32[192]{0:T(256)S(1)} %multiply_add_fusion), kind=kOutput, calls=%fused_computation.1 | convolution fusion | flops 1815250944 | bytes 15729408 | tf_op jit(solution)/shard_map/dot_general | solution.py:63
  776.8 6.5 reduce_sum.39
  (35 shorter events, 10.6 us)
Async XLA Ops:
  7.2 215.5 %all-reduce.2.cloned.1.call-start = ((), (), s32[]{:S(2)}) async-start(), calls=%async_computation.1 | async-start | bytes 12582912 | tf_op jit(solution)/shard_map/psum | solution.py:47
  7.2 0.7 copy-start.8
  236.9 14.0 %copy-start = (f32[1,36,16384]{2,0,1:T(1,128)S(1)}, f32[1,36,16384]{2,0,1:T(1,128)}, u32[]{:S(2)}) copy-start(f32[1,36,16384]{2,0,1:T(1,128)} %param.11) | copy-start | bytes 7077892
  259.4 517.4 %all-to-all-start = ((f32[8,24,16384]{2,1,0:T(8,128)}), f32[8,24,16384]{2,1,0:T(8,128)}, u32[]{:S(2)}, u32[]{:S(2)}) async-start(f32[8,24,16384]{2,1,0:T(8,128)} %bitcast.43), calls=%async_computation | async-start | bytes 25165824 | tf_op jit(solution)/shard_map/all_to_all | solution.py:70
  266.7 232.8 %collective-permute-start = (bf16[36,16384]{1,0:T(8,128)(2,1)}, bf16[36,16384]{1,0:T(8,128)(2,1)S(1)}, u32[]{:S(2)}, u32[]{:S(2)}) collective-permute-start(bf16[36,16384]{1,0:T(8,128)(2,1)} %get-tuple-element.15), channel_id=1, source_target_pairs={{0,4},{4,8},{8,12},{12,16},{16,20},{20,24},{24,28},{28,0},{1,5},{5... | collective-permute-start | bytes 3538952 | tf_op jit(solution)/shard_map/ppermute | solution.py:14
  268.2 298.9 %collective-permute-start.1 = (bf16[36,16384]{1,0:T(8,128)(2,1)}, bf16[36,16384]{1,0:T(8,128)(2,1)S(1)}, u32[]{:S(2)}, u32[]{:S(2)}) collective-permute-start(bf16[36,16384]{1,0:T(8,128)(2,1)} %get-tuple-element.15), channel_id=1, source_target_pairs={{0,28},{4,0},{8,4},{12,8},{16,12},{20,16},{24,20},{28,24},{1,29},{... | collective-permute-start | bytes 3538952 | tf_op jit(solution)/shard_map/ppermute | solution.py:17
  499.5 1.1 copy-start.3
  500.6 122.8 %collective-permute-start.2 = (bf16[36,16384]{1,0:T(8,128)(2,1)S(1)}, bf16[36,16384]{1,0:T(8,128)(2,1)S(1)}, u32[]{:S(2)}, u32[]{:S(2)}) collective-permute-start(bf16[36,16384]{1,0:T(8,128)(2,1)S(1)} %collective-permute-done), channel_id=1, source_target_pairs={{0,4},{4,8},{8,12},{12,16},{16,20},{20,24},{24,28},{28,0},{1,5},{5... | collective-permute-start | bytes 3538952 | tf_op jit(solution)/shard_map/ppermute | solution.py:14
  567.1 56.3 %copy-start.4 = (bf16[36,16384]{1,0:T(8,128)(2,1)}, bf16[36,16384]{1,0:T(8,128)(2,1)S(1)}, u32[]{:S(2)}) copy-start(bf16[36,16384]{1,0:T(8,128)(2,1)S(1)} %collective-permute-done.1) | copy-start | bytes 3538948
  567.1 58.8 %collective-permute-start.3 = (bf16[36,16384]{1,0:T(8,128)(2,1)S(1)}, bf16[36,16384]{1,0:T(8,128)(2,1)}, u32[]{:S(2)}, u32[]{:S(2)}) collective-permute-start(bf16[36,16384]{1,0:T(8,128)(2,1)S(1)} %collective-permute-done.1), channel_id=1, source_target_pairs={{0,28},{4,0},{8,4},{12,8},{16,12},{20,16},{24,20},{28,24},{1,29},{... | collective-permute-start | bytes 3538952 | tf_op jit(solution)/shard_map/ppermute | solution.py:17
  623.4 2.5 copy-start.6
  623.4 57.9 %collective-permute-start.4 = (bf16[36,16384]{1,0:T(8,128)(2,1)S(1)}, bf16[36,16384]{1,0:T(8,128)(2,1)}, u32[]{:S(2)}, u32[]{:S(2)}) collective-permute-start(bf16[36,16384]{1,0:T(8,128)(2,1)S(1)} %collective-permute-done.2), channel_id=1, source_target_pairs={{0,4},{4,8},{8,12},{12,16},{16,20},{20,24},{24,28},{28,0},{1,5},{5... | collective-permute-start | bytes 3538952 | tf_op jit(solution)/shard_map/ppermute | solution.py:14
  625.9 123.9 %collective-permute-start.5 = (bf16[36,16384]{1,0:T(8,128)(2,1)}, bf16[36,16384]{1,0:T(8,128)(2,1)}, u32[]{:S(2)}, u32[]{:S(2)}) collective-permute-start(bf16[36,16384]{1,0:T(8,128)(2,1)} %collective-permute-done.3), channel_id=1, source_target_pairs={{0,28},{4,0},{8,4},{12,8},{16,12},{20,16},{24,20},{28,24},{1,29},{... | collective-permute-start | bytes 3538952 | tf_op jit(solution)/shard_map/ppermute | solution.py:17
  681.3 77.0 %collective-permute-start.6 = (bf16[36,16384]{1,0:T(8,128)(2,1)}, bf16[36,16384]{1,0:T(8,128)(2,1)}, u32[]{:S(2)}, u32[]{:S(2)}) collective-permute-start(bf16[36,16384]{1,0:T(8,128)(2,1)} %collective-permute-done.4), channel_id=1, source_target_pairs={{0,4},{4,8},{8,12},{12,16},{16,20},{20,24},{24,28},{28,0},{1,5},{5... | collective-permute-start | bytes 3538952 | tf_op jit(solution)/shard_map/ppermute | solution.py:14
  697.2 3.8 copy-start.2
  701.0 3.8 copy-start.1
  708.7 8.7 %copy-start.5 = (bf16[36,16384]{1,0:T(8,128)(2,1)S(1)}, bf16[36,16384]{1,0:T(8,128)(2,1)}, u32[]{:S(2)}) copy-start(bf16[36,16384]{1,0:T(8,128)(2,1)} %copy-done.4) | copy-start | bytes 3538948
  708.7 16.7 %copy-start.7 = (bf16[36,16384]{1,0:T(8,128)(2,1)S(1)}, bf16[36,16384]{1,0:T(8,128)(2,1)}, u32[]{:S(2)}) copy-start(bf16[36,16384]{1,0:T(8,128)(2,1)} %copy-done.6) | copy-start | bytes 3538948
Sparse Core Ops, SparseCore 0:
  11.8 210.8 all-reduce.1
